TPU v7x, 256 devices: a whole 4x4x8 slice. The times are simulated.
256 devices in a mesh: tok: 64 (over y, z, core), head: 4 (over x).
Axes of the slice: x: 4, y: 4, z: 8, core: 2. Of those that a mesh axis runs over, the one named last changes fastest.
Arguments:
- hidden: bfloat16 [2048, 2048], P('tok', 'head'), may hold values from -24 to 24
- attn_gain: float32 [2048], replicated, may hold values from 0.1 to 1.9
- w_query: bfloat16 [2048, 3072], P(None, 'head'), may hold values from -0.125 to 0.125
- w_latent: bfloat16 [2048, 576], P('head'), may hold values from -0.125 to 0.125
- w_key_up: bfloat16 [16, 128, 512], P('head'), may hold values from -0.5 to 0.5
- w_value_up: bfloat16 [16, 512, 128], P('head'), may hold values from -1 to 1
- w_out: bfloat16 [2048, 2048], P('head'), may hold values from -0.125 to 0.125
- latent_cache: bfloat16 [638976, 576], P(('tok', 'head')), may hold values from -6 to 6
- cache_lengths: int32 [2048], P('tok'), may hold values from 144 to 2048, as said below
- request_slot: int32 [2048], P('tok'), may hold values from 0 to 2047, as said below
- ffn_gain: float32 [2048], P('head'), may hold values from 0.1 to 1.9
- w_router: bfloat16 [2048, 64], P('head'), may hold values from -0.25 to 0.25
- routes: int32 [2048, 6], P('tok'), may hold values from 0 to 63, all different within a row; in each aligned block of 32 rows (0 to 31, 32 to 63, ...) at most 6 rows name the same one
- expert_gate: bfloat16 [64, 2048, 1408], P('tok', None, 'head'), may hold values from -0.125 to 0.125
- expert_up: bfloat16 [64, 2048, 1408], P('tok', None, 'head'), may hold values from -0.125 to 0.125
- expert_down: bfloat16 [64, 1408, 2048], P('tok', 'head'), may hold values from -0.15625 to 0.15625
Outputs:
- new_entry: bfloat16 [2048, 576], P('tok')
- attended: bfloat16 [2048, 2048], P('tok', 'head')
- expert_mix: bfloat16 [2048, 2048], P('tok', 'head')
Inputs may be any that keep to these rules, and one draw needn't show every extreme that they name: `request_slot`: a permutation of the 2048 slots; slot s lies on owner s // 32, so every owner holds 32 slots; the requests of one device name at most 1 slots of one owner, and every device reaches that bound. `cache_lengths`: the caches of an owner's slots lie end to end in slot order at the start of that owner's 9984 rows of latent_cache; they fill at most 9984 rows, and some owner fills all of them. `routes`: each row names 6 different experts; in the rows of one device no expert is named more than 6 times.
All inputs are finite; a program needn't handle non-finite values.
Results may differ from a plain program's by a relative error of at most 0.028.
Values may be sent and summed in bfloat16 or wider, within the bound.
No kernel may reach another device: no remote copies, remote signals or barrier semaphores. Data moves between devices by JAX's collectives and lax.ppermute only.
A program may use at most 128 MiB of HBM per device.

v0:
```python
import jax
import jax.numpy as jnp
from jax import lax
from jax.sharding import PartitionSpec as P

D = 2048
NOPE = 128
ROPE = 64
LATENT = 512
NORM_EPS = 1e-06


def rotate_pairs(values, places):
    halfway = values.shape[-1] // 2
    freqs = 10000.0 ** (-jnp.arange(halfway, dtype=jnp.float32) / halfway)
    angles = places.astype(jnp.float32).reshape(places.shape + (1,) * (values.ndim - 1)) * freqs
    cosine = jnp.cos(angles)
    sine = jnp.sin(angles)
    first_half = values[..., :halfway]
    second_half = values[..., halfway:]
    return jnp.concatenate(
        [first_half * cosine - second_half * sine, first_half * sine + second_half * cosine],
        axis=-1,
    )


def owner_attend(all_heads, owner_lengths, latent_cache, head_index, factor):
    slot_rows = all_heads.shape[0]
    total_heads = all_heads.shape[1]
    probe_width = all_heads.shape[2]
    key_rows = latent_cache.shape[0]
    starts = jnp.cumsum(owner_lengths) - owner_lengths
    places = head_index * key_rows + jnp.arange(key_rows, dtype=jnp.int32)
    inside = (places[None, :] >= starts[:, None]) & (
        places[None, :] < (starts + owner_lengths)[:, None]
    )
    scores = factor * jnp.einsum(
        "qc,pc->qp",
        all_heads.reshape(slot_rows * total_heads, probe_width),
        latent_cache,
        preferred_element_type=jnp.float32,
    )
    scores = scores.reshape(slot_rows, total_heads, key_rows)
    weights = jnp.where(inside[:, None, :], jnp.exp(scores), 0.0).astype(jnp.bfloat16)
    numerator = jnp.einsum(
        "khp,pl->khl", weights, latent_cache[:, :LATENT], preferred_element_type=jnp.float32
    )
    denominator = jnp.sum(weights.astype(jnp.float32), axis=2)
    return (numerator, denominator)


def body(
    hidden,
    attn_gain,
    w_query,
    w_latent,
    w_key_up,
    w_value_up,
    w_out,
    latent_cache,
    cache_lengths,
    request_slot,
    ffn_gain,
    w_router,
    routes,
    expert_gate,
    expert_up,
    expert_down,
):
    local_rows = hidden.shape[0]
    quarter_width = hidden.shape[1]
    local_heads = w_key_up.shape[0]
    peer_count = lax.axis_size("tok")
    head_index = lax.axis_index("head")
    tok_index = lax.axis_index("tok")
    row_ids = jnp.arange(local_rows, dtype=jnp.int32)
    gathered = lax.all_gather(hidden, "head", axis=1, tiled=True)
    widened = gathered.astype(jnp.float32)
    inv_attn = lax.rsqrt(jnp.mean(widened * widened, axis=1, keepdims=True) + NORM_EPS)
    normed_attn = (widened * inv_attn * attn_gain).astype(jnp.bfloat16)
    normed_part = lax.dynamic_slice_in_dim(
        normed_attn, head_index * quarter_width, quarter_width, 1
    )
    compressed = lax.psum(
        jnp.dot(normed_part, w_latent, preferred_element_type=jnp.float32), "head"
    )
    latent_new = compressed[:, :LATENT]
    latent_new = latent_new * lax.rsqrt(
        jnp.mean(latent_new * latent_new, axis=1, keepdims=True) + NORM_EPS
    )
    new_entry = jnp.concatenate(
        [latent_new, rotate_pairs(compressed[:, LATENT:], cache_lengths)], axis=1
    ).astype(jnp.bfloat16)
    queries = jnp.dot(normed_attn, w_query, preferred_element_type=jnp.float32).astype(jnp.bfloat16)
    queries = queries.reshape(local_rows, local_heads, NOPE + ROPE)
    absorbed = jnp.einsum(
        "bhn,hnl->bhl", queries[:, :, :NOPE], w_key_up, preferred_element_type=jnp.float32
    ).astype(jnp.bfloat16)
    turned = rotate_pairs(queries[:, :, NOPE:].astype(jnp.float32), cache_lengths).astype(
        jnp.bfloat16
    )
    probes = jnp.concatenate([absorbed, turned], axis=2)
    factor = (NOPE + ROPE) ** (-0.5)
    owner_ids = jnp.arange(peer_count, dtype=jnp.int32)
    dest_owner = request_slot // local_rows
    goes_to = dest_owner[None, :] == owner_ids[:, None]
    sent_any = jnp.max(goes_to.astype(jnp.int32), axis=1)
    sent_row = jnp.sum(jnp.where(goes_to, row_ids[None, :], 0), axis=1) + local_rows * (
        1 - sent_any
    )
    packed = jnp.concatenate([probes, new_entry[:, None, :]], axis=1)
    packed = jnp.concatenate([packed, jnp.zeros((1,) + packed.shape[1:], jnp.bfloat16)], axis=0)
    send_ints = jnp.stack(
        [
            jnp.where(sent_any > 0, request_slot[jnp.minimum(sent_row, local_rows - 1)], -1),
            cache_lengths[jnp.minimum(sent_row, local_rows - 1)],
        ],
        axis=1,
    )
    got_packed = lax.all_to_all(packed[sent_row], "tok", 0, 0, tiled=True)
    got_ints = lax.all_to_all(send_ints, "tok", 0, 0, tiled=True)
    got_slot = got_ints[:, 0]
    local_slot = got_slot - tok_index * local_rows
    slot_sel = local_slot[None, :] == row_ids[:, None]
    src_of_slot = jnp.sum(jnp.where(slot_sel, owner_ids[None, :], 0), axis=1)
    owner_packed = got_packed[src_of_slot]
    owner_probes = owner_packed[:, :local_heads]
    owner_new = owner_packed[:, local_heads]
    owner_lengths = got_ints[src_of_slot, 1]
    all_heads = lax.all_gather(owner_probes, "head", axis=1, tiled=True)
    numerator, denominator = owner_attend(
        all_heads, owner_lengths, latent_cache, head_index, factor
    )
    joined = lax.psum_scatter(
        jnp.concatenate([numerator, denominator[:, :, None]], axis=2),
        "head",
        scatter_dimension=1,
        tiled=True,
    )
    group_num = joined[:, :, :LATENT]
    group_den = joined[:, :, LATENT]
    self_score = factor * jnp.einsum(
        "bhc,bc->bh", owner_probes, owner_new, preferred_element_type=jnp.float32
    )
    self_weight = jnp.exp(self_score).astype(jnp.bfloat16).astype(jnp.float32)
    total_num = group_num + self_weight[:, :, None] * owner_new[:, None, :LATENT].astype(
        jnp.float32
    )
    total_den = group_den + self_weight
    mixed_latent = (total_num / total_den[:, :, None]).astype(jnp.bfloat16)
    owner_out = jnp.einsum(
        "bhl,hld->bhd", mixed_latent, w_value_up, preferred_element_type=jnp.float32
    ).astype(jnp.bfloat16)
    owner_out = owner_out.reshape(local_rows, local_heads * NOPE)
    owner_out = jnp.concatenate(
        [owner_out, jnp.zeros((1, local_heads * NOPE), jnp.bfloat16)], axis=0
    )
    back_valid = (local_slot >= 0) & (local_slot < local_rows)
    back_row = jnp.where(back_valid, local_slot, local_rows)
    returned_out = lax.all_to_all(owner_out[back_row], "tok", 0, 0, tiled=True)
    head_out = returned_out[dest_owner]
    head_out = head_out.reshape(local_rows, local_heads * NOPE)
    attn_piece = lax.psum_scatter(
        jnp.dot(head_out, w_out, preferred_element_type=jnp.float32),
        "head",
        scatter_dimension=1,
        tiled=True,
    )
    attended = (hidden.astype(jnp.float32) + attn_piece).astype(jnp.bfloat16)
    attended_wide = attended.astype(jnp.float32)
    gained = (attended_wide * ffn_gain).astype(jnp.bfloat16)
    squares, logit_part = lax.psum(
        (
            jnp.sum(attended_wide * attended_wide, axis=1),
            jnp.dot(gained, w_router, preferred_element_type=jnp.float32),
        ),
        "head",
    )
    inv_ffn = lax.rsqrt(squares / D + NORM_EPS)
    logits = logit_part * inv_ffn[:, None]
    normed_ffn = (attended_wide * ffn_gain * inv_ffn[:, None]).astype(jnp.bfloat16)
    expert_count = w_router.shape[1]
    route_count = routes.shape[1]
    expert_ids = jnp.arange(expert_count, dtype=jnp.int32)
    named = routes[:, :, None] == expert_ids[None, None, :]
    picked = jnp.sum(jnp.where(named, logits[:, None, :], 0.0), axis=2)
    lifted = jnp.exp(picked)
    route_weight = lifted / jnp.sum(lifted, axis=1, keepdims=True)
    struck = jnp.max(named.astype(jnp.int32), axis=1)
    earlier_hits = jnp.cumsum(struck, axis=0) - struck
    capacity = min(local_rows, max(2, 2 * local_rows * route_count // expert_count))
    route_place = routes * capacity + jnp.take_along_axis(earlier_hits, routes, axis=1)
    slot_total = expert_count * capacity
    slot_ids = jnp.arange(slot_total, dtype=jnp.int32)
    filled = route_place[None, :, :] == slot_ids[:, None, None]
    source_token = jnp.sum(
        jnp.where(filled, row_ids[None, :, None], 0), axis=(1, 2)
    ) + local_rows * (1 - jnp.max(filled.astype(jnp.int32), axis=(1, 2)))
    full_rows = lax.all_gather(normed_ffn, "head", axis=1, tiled=True)
    padded_rows = jnp.concatenate(
        [full_rows, jnp.zeros((1, full_rows.shape[1]), jnp.bfloat16)], axis=0
    )
    arrived = lax.all_to_all(
        padded_rows[source_token].reshape(expert_count, capacity, full_rows.shape[1]),
        "tok",
        split_axis=0,
        concat_axis=0,
        tiled=True,
    )
    expert_in = arrived.reshape(peer_count * capacity, full_rows.shape[1])
    gate_value = jnp.dot(expert_in, expert_gate[0], preferred_element_type=jnp.float32)
    up_value = jnp.dot(expert_in, expert_up[0], preferred_element_type=jnp.float32)
    activity = (jax.nn.silu(gate_value) * up_value).astype(jnp.bfloat16)
    expert_share = lax.psum_scatter(
        jnp.dot(activity, expert_down[0], preferred_element_type=jnp.float32).astype(jnp.bfloat16),
        "head",
        scatter_dimension=1,
        tiled=True,
    )
    returned = lax.all_to_all(
        expert_share.reshape(peer_count, capacity, quarter_width),
        "tok",
        split_axis=0,
        concat_axis=0,
        tiled=True,
    )
    chosen_rows = returned.reshape(slot_total, quarter_width)[route_place]
    expert_mix = jnp.sum(route_weight[:, :, None] * chosen_rows.astype(jnp.float32), axis=1).astype(
        jnp.bfloat16
    )
    return (new_entry, attended, expert_mix)


def solution(mesh):
    in_specs = (
        P("tok", "head"),
        P(),
        P(None, "head"),
        P("head", None),
        P("head", None, None),
        P("head", None, None),
        P("head", None),
        P(("tok", "head"), None),
        P("tok"),
        P("tok"),
        P("head"),
        P("head", None),
        P("tok", None),
        P("tok", None, "head"),
        P("tok", None, "head"),
        P("tok", "head", None),
    )
    out_specs = (P("tok", None), P("tok", "head"), P("tok", "head"))
    return jax.shard_map(body, mesh=mesh, in_specs=in_specs, out_specs=out_specs, check_vma=False)
```

profile of v0, /device:TPU:1, one launch (start us, length us, event | category | flops | bytes accessed | tf_op | source)
XLA Modules:
  0.0 402.8 jit_solution(13905377801501472798)
XLA Ops:
  7.2 1.4 compare_select_fusion.3
  8.7 1.4 gather_fusion
  10.1 1.4 gather_fusion.1
  11.6 0.7 copy.107
  12.3 13.1 %all-to-all-start = ((s32[64,1,2]{2,1,0:T(1,128)}), s32[64,1,2]{2,1,0:T(1,128)S(1)}, u32[]{:S(2)}, u32[]{:S(2)}) async-start(s32[64,1,2]{2,1,0:T(1,128)} %copy.107), calls=%async_computation | async-start | bytes 65536 | tf_op jit(solution)/shard_map/all_to_all | solution.py:121
  25.5 10.3 %all_gather.9 = bf16[32,2048]{1,0:T(8,128)(2,1)S(1)} all-gather(bf16[32,512]{1,0:T(8,128)(2,1)} %param.16), channel_id=1, replica_groups=mesh['tok'=64,'head'=4] {'head'}, dimensions={1}, use_global_device_ids=true | all-gather | bytes 163840 | tf_op jit(solution)/shard_map/all_gather | solution.py:77
  35.9 0.8 fusion.28
  36.7 2.0 fusion.45
  38.8 0.6 convolution_convert_fusion.2
  39.6 0.6 iota_add_fusion
  40.2 1.2 fusion.16
  42.7 0.8 gather_fusion.2
  44.3 40.8 %all-reduce.7.cloned.1.call-done = f32[32,576]{1,0:T(8,128)} async-done(((f32[32,576]{1,0:T(8,128)}), f32[32,576]{1,0:T(8,128)}) %all-reduce.7.cloned.1.call-update) | async-done | bytes 73744 | tf_op jit(solution)/shard_map/psum | solution.py:84
  85.1 1.0 multiply_reduce_fusion.1
  86.0 0.9 multiply_cosine_fusion
  87.1 0.9 fusion.76
  88.3 1.5 gather_fusion.3
  89.8 13.0 %all-to-all-start.1 = ((bf16[64,5,576]{2,1,0:T(8,128)(2,1)}), bf16[64,5,576]{2,1,0:T(8,128)(2,1)}, u32[]{:S(2)}, u32[]{:S(2)}) async-start(bf16[64,5,576]{2,1,0:T(8,128)(2,1)} %gather_fusion.3), calls=%async_computation.1 | async-start | bytes 1310720 | tf_op jit(solution)/shard_map/all_to_all | solution.py:120
  102.8 0.8 compare_and_fusion
  104.0 2.5 copy.117
  106.5 0.6 pad_clamp_fusion.4
  107.1 15.7 %all-to-all-done.1 = bf16[64,5,576]{2,1,0:T(8,128)(2,1)} async-done(((bf16[64,5,576]{2,1,0:T(8,128)(2,1)}), bf16[64,5,576]{2,1,0:T(8,128)(2,1)}, u32[]{:S(2)}, u32[]{:S(2)}) %all-to-all-start.1) | async-done | bytes 368672 | tf_op jit(solution)/shard_map/all_to_all | solution.py:120
  122.8 1.8 gather_fusion.4
  124.7 0.6 copy-done.5
  125.3 11.3 %all_gather.10 = bf16[32,16,576]{2,0,1:T(8,128)(2,1)S(1)} all-gather(bf16[32,4,576]{2,0,1:T(8,128)(2,1)S(1)} %copy.113), channel_id=1, replica_groups=mesh['tok'=64,'head'=4] {'head'}, dimensions={1}, use_global_device_ids=true | all-gather | bytes 737280 | tf_op jit(solution)/shard_map/all_gather | solution.py:130
  136.9 6.9 %convert_reduce_fusion = (f32[512]{0:T(512)}, bf16[512,2496]{0,1:T(8,128)(2,1)}) fusion(pred[512,2496]{0,1:T(32,128)(4,1)S(1)} %copy-done.2, bf16[512,576]{1,0:T(8,128)(2,1)S(1)} %bitcast.106, bf16[2496,576]{0,1:T(8,128)(2,1)} %param.23), kind=kOutput, calls=%fused_computation.11 | convolution fusion | flops 1478589952 | bytes 7301120 | tf_op jit(solution)/shard_map/qc,pc->qp/dot_general | solution.py:37
  143.8 0.9 broadcast_in_dim.142
  144.7 4.4 %copy.115 = bf16[512,2496]{1,0:T(8,128)(2,1)} copy(bf16[512,2496]{0,1:T(8,128)(2,1)} %get-tuple-element.32) | data formatting | bytes 5111808 | tf_op jit(solution)/shard_map/exp | solution.py:44
  149.1 4.1 %fusion = f32[32,16,512]{2,1,0:T(8,128)S(1)} fusion(bf16[32,16,2496]{2,1,0:T(8,128)(2,1)} %bitcast.104, bf16[2496,576]{0,1:T(8,128)(2,1)} %param.23, pred[32,2496]{1,0:T(8,128)(4,1)S(1)} %compare_and_fusion), kind=kOutput, calls=%fused_computation.15 | convolution fusion | flops 1309900800 | bytes 6371328 | tf_op jit(solution)/shard_map/khp,pl->khl/dot_general | solution.py:45
  153.4 1.5 copy.119
  155.1 1.8 fusion.35
  157.0 0.8 copy.129
  157.8 21.0 %reduce-scatter.4.cloned.1.call-done = f32[32,4,513]{2,0,1:T(8,128)} async-done(((f32[32,16,513]{2,0,1:T(8,128)}), f32[32,4,513]{2,0,1:T(8,128)}) %reduce-scatter.4.cloned.1.call-update) | async-done | bytes 262672 | tf_op jit(solution)/shard_map/reduce_scatter | solution.py:134
  178.8 0.9 slice_reduce_fusion
  179.7 1.4 fusion.17
  181.2 0.7 gather_fusion.5
  182.4 0.7 reduce.6
  183.0 0.6 reshape.501
  183.7 12.9 %all-to-all-start.2 = ((bf16[64,2,256]{2,1,0:T(2,128)(2,1)}), bf16[64,2,256]{2,1,0:T(2,128)(2,1)S(1)}, u32[]{:S(2)}, u32[]{:S(2)}) async-start(bf16[64,2,256]{2,1,0:T(2,128)(2,1)} %reshape.501), calls=%async_computation.3 | async-start | bytes 131072 | tf_op jit(solution)/shard_map/all_to_all | solution.py:160
  197.0 1.6 gather_fusion.9
  198.7 7.7 %all-to-all-done.2 = bf16[64,2,256]{2,1,0:T(2,128)(2,1)S(1)} async-done(((bf16[64,2,256]{2,1,0:T(2,128)(2,1)}), bf16[64,2,256]{2,1,0:T(2,128)(2,1)S(1)}, u32[]{:S(2)}, u32[]{:S(2)}) %all-to-all-start.2) | async-done | bytes 65568 | tf_op jit(solution)/shard_map/all_to_all | solution.py:160
  206.5 0.6 gather_fusion.6
  207.2 2.8 fusion.62
  210.3 14.0 %reduce-scatter.6.cloned.1.call-done = f32[32,512]{1,0:T(8,128)} async-done(((f32[32,2048]{1,0:T(8,128)}), f32[32,512]{1,0:T(8,128)}) %reduce-scatter.6.cloned.1.call-update) | async-done | bytes 65552 | tf_op jit(solution)/shard_map/reduce_scatter | solution.py:163
  224.3 1.0 fusion.40
  225.4 11.8 %all-reduce.4 = (f32[32]{0:T(128)S(1)}, f32[32,64]{1,0:T(8,128)S(1)}) all-reduce(f32[32]{0:T(128)S(1)} %get-tuple-element.11, f32[32,64]{1,0:T(8,128)S(1)} %fusion.41), channel_id=1, replica_groups=mesh['tok'=64,'head'=4] {'head'}, use_global_device_ids=true, to_apply=%region_12.13 | all-reduce | flops 2080 | bytes 16640 | tf_op jit(solution)/shard_map/psum | solution.py:172
  237.3 9.1 %all_gather.11 = bf16[32,2048]{1,0:T(8,128)(2,1)S(1)} all-gather(bf16[32,512]{1,0:T(8,128)(2,1)S(1)} %fusion.39), channel_id=1, replica_groups=mesh['tok'=64,'head'=4] {'head'}, dimensions={1}, use_global_device_ids=true | all-gather | bytes 163840 | tf_op jit(solution)/shard_map/all_gather | solution.py:199
  246.4 3.1 gather_fusion.7
  249.5 3.7 reshape.405
  253.2 70.5 %all_to_all.39 = bf16[64,6,2048]{2,1,0:T(8,128)(2,1)} all-to-all(bf16[64,6,2048]{2,1,0:T(8,128)(2,1)} %reshape.405), channel_id=1, replica_groups=mesh['tok'=64,'head'=4] {'tok'}, dimensions={0} | all-to-all | bytes 3145728 | tf_op jit(solution)/shard_map/all_to_all | solution.py:203
  323.7 3.7 reshape.406
  327.4 3.6 fusion.8
  331.0 5.5 %convolution_convert_fusion = bf16[384,2048]{1,0:T(8,128)(2,1)} fusion(bf16[1,352,2048]{2,1,0:T(8,128)(2,1)} %param.31, bf16[384,2048]{1,0:T(8,128)(2,1)} %reshape.406, bf16[1,2048,352]{1,2,0:T(8,128)(2,1)} %param.30, f32[384,352]{0,1:T(8,128)} %fusion.8), kind=kOutput, calls=%fused_computation.14 | convolution fusion | flops 1108893696 | bytes 6569984 | tf_op jit(solution)/shard_map/dot_general | solution.py:215
  336.6 0.7 copy-done.6
  337.4 21.5 %reduce-scatter.8.cloned.1.call-done = bf16[384,512]{1,0:T(8,128)(2,1)} async-done(((bf16[384,2048]{1,0:T(8,128)(2,1)}), bf16[384,512]{1,0:T(8,128)(2,1)}) %reduce-scatter.8.cloned.1.call-update) | async-done | bytes 393232 | tf_op jit(solution)/shard_map/reduce_scatter | solution.py:214
  359.0 1.9 reshape.407
  360.9 11.7 %all-to-all-start.4 = ((bf16[64,6,512]{2,1,0:T(8,128)(2,1)}), bf16[64,6,512]{2,1,0:T(8,128)(2,1)}, u32[]{:S(2)}, u32[]{:S(2)}) async-start(bf16[64,6,512]{2,1,0:T(8,128)(2,1)} %reshape.407), calls=%async_computation.7 | async-start | bytes 1048576 | tf_op jit(solution)/shard_map/all_to_all | solution.py:220
  372.6 0.7 pad_maximum_fusion.1
  373.6 0.7 copy.122
  374.3 15.5 %all-to-all-done.4 = bf16[64,6,512]{2,1,0:T(8,128)(2,1)} async-done(((bf16[64,6,512]{2,1,0:T(8,128)(2,1)}), bf16[64,6,512]{2,1,0:T(8,128)(2,1)}, u32[]{:S(2)}, u32[]{:S(2)}) %all-to-all-start.4) | async-done | bytes 393248 | tf_op jit(solution)/shard_map/all_to_all | solution.py:220
  389.8 1.2 reshape.408
  390.9 1.7 gather_fusion.8
  392.6 1.8 reshape.488
  394.4 1.9 multiply_reduce_fusion
  (118 shorter events, 6.0 us)
Async XLA Ops:
  7.2 31.6 %copy-start = (bf16[2048,768]{1,0:T(8,128)(2,1)S(1)}, bf16[2048,768]{1,0:T(8,128)(2,1)}, u32[]{:S(2)}) copy-start(bf16[2048,768]{1,0:T(8,128)(2,1)} %param.18) | copy-start | bytes 9437188
  12.3 29.2 %all-to-all-start = ((s32[64,1,2]{2,1,0:T(1,128)}), s32[64,1,2]{2,1,0:T(1,128)S(1)}, u32[]{:S(2)}, u32[]{:S(2)}) async-start(s32[64,1,2]{2,1,0:T(1,128)} %copy.107), calls=%async_computation | async-start | bytes 65536 | tf_op jit(solution)/shard_map/all_to_all | solution.py:121
  25.5 59.6 %all-reduce.7.cloned.1.call-start = ((), (), s32[]{:S(2)}) async-start(), calls=%async_computation.8 | async-start | bytes 163840 | tf_op jit(solution)/shard_map/psum | solution.py:84
  38.7 2.7 copy-start.1
  43.7 44.4 %copy-start.18 = (s32[32]{0:T(128)}, s32[32]{0:T(128)S(1)}, u32[]{:S(2)}) copy-start(s32[32]{0:T(128)S(1)} %reduce.1) | copy-start | bytes 388
  86.0 2.1 copy-start.16
  87.0 1.0 copy-start.9
  87.0 1.0 copy-start.11
  89.8 33.0 %all-to-all-start.1 = ((bf16[64,5,576]{2,1,0:T(8,128)(2,1)}), bf16[64,5,576]{2,1,0:T(8,128)(2,1)}, u32[]{:S(2)}, u32[]{:S(2)}) async-start(bf16[64,5,576]{2,1,0:T(8,128)(2,1)} %gather_fusion.3), calls=%async_computation.1 | async-start | bytes 1310720 | tf_op jit(solution)/shard_map/all_to_all | solution.py:120
  102.7 76.0 %reduce-scatter.4.cloned.1.call-start = ((), (), s32[]{:S(2)}) async-start(), calls=%async_computation.9 | async-start | bytes 1638400 | tf_op jit(solution)/shard_map/reduce_scatter | solution.py:134
  104.0 2.5 copy-start.21
  124.6 19.2 %copy-start.3 = (bf16[32,5,576]{2,1,0:T(8,128)(2,1)}, bf16[32,5,576]{2,1,0:T(8,128)(2,1)S(1)}, u32[]{:S(2)}) copy-start(bf16[32,5,576]{2,1,0:T(8,128)(2,1)S(1)} %gather_fusion.4) | copy-start | bytes 552964
  124.6 12.3 %copy-start.2 = (pred[512,2496]{0,1:T(32,128)(4,1)S(1)}, pred[512,2496]{0,1:T(32,128)(4,1)}, u32[]{:S(2)}) copy-start(pred[512,2496]{0,1:T(32,128)(4,1)} %copy.117) | copy-start | bytes 3833860
  124.7 0.7 copy-start.5
  153.4 1.5 copy-start.14
  153.4 1.6 copy-start.19
  153.4 1.6 copy-start.4
  183.7 22.7 %all-to-all-start.2 = ((bf16[64,2,256]{2,1,0:T(2,128)(2,1)}), bf16[64,2,256]{2,1,0:T(2,128)(2,1)S(1)}, u32[]{:S(2)}, u32[]{:S(2)}) async-start(bf16[64,2,256]{2,1,0:T(2,128)(2,1)} %reshape.501), calls=%async_computation.3 | async-start | bytes 131072 | tf_op jit(solution)/shard_map/all_to_all | solution.py:160
  196.6 27.7 %reduce-scatter.6.cloned.1.call-start = ((), (), s32[]{:S(2)}) async-start(), calls=%async_computation.10 | async-start | bytes 327680 | tf_op jit(solution)/shard_map/reduce_scatter | solution.py:163
  196.9 1.7 copy-start.20
  206.5 17.8 %copy-start.8 = (bf16[32,512]{1,0:T(8,128)(2,1)S(1)}, bf16[32,512]{1,0:T(8,128)(2,1)}, u32[]{:S(2)}) copy-start(bf16[32,512]{1,0:T(8,128)(2,1)} %param.16) | copy-start | bytes 98308
  206.5 18.8 %copy-start.13 = (bf16[512,64]{0,1:T(8,128)(2,1)S(1)}, bf16[512,64]{0,1:T(8,128)(2,1)}, u32[]{:S(2)}) copy-start(bf16[512,64]{0,1:T(8,128)(2,1)} %param.27) | copy-start | bytes 196612
  206.5 18.8 %copy-start.15 = (f32[512]{0:T(512)S(1)}, f32[512]{0:T(512)}, u32[]{:S(2)}) copy-start(f32[512]{0:T(512)} %param.26) | copy-start | bytes 6148
  209.9 149.0 %reduce-scatter.8.cloned.1.call-start = ((), (), s32[]{:S(2)}) async-start(), calls=%async_computation.11 | async-start | bytes 1966080 | tf_op jit(solution)/shard_map/reduce_scatter | solution.py:214
  225.3 12.0 %copy-start.7 = (bf16[32,512]{1,0:T(8,128)(2,1)}, bf16[32,512]{1,0:T(8,128)(2,1)S(1)}, u32[]{:S(2)}) copy-start(bf16[32,512]{1,0:T(8,128)(2,1)S(1)} %get-tuple-element.12) | copy-start | bytes 98308
  336.5 0.9 copy-start.6
  336.5 0.9 copy-start.17
  336.5 36.1 %copy-start.10 = (bf16[32,32]{1,0:T(8,128)(2,1)S(1)}, bf16[32,32]{1,0:T(8,128)(2,1)}, u32[]{:S(2)}) copy-start(bf16[32,32]{1,0:T(8,128)(2,1)} %copy-done.9) | copy-start | bytes 6148
  336.5 36.1 %copy-start.12 = (bf16[32,32]{1,0:T(8,128)(2,1)S(1)}, bf16[32,32]{1,0:T(8,128)(2,1)}, u32[]{:S(2)}) copy-start(bf16[32,32]{1,0:T(8,128)(2,1)} %copy-done.11) | copy-start | bytes 6148
  360.9 28.9 %all-to-all-start.4 = ((bf16[64,6,512]{2,1,0:T(8,128)(2,1)}), bf16[64,6,512]{2,1,0:T(8,128)(2,1)}, u32[]{:S(2)}, u32[]{:S(2)}) async-start(bf16[64,6,512]{2,1,0:T(8,128)(2,1)} %reshape.407), calls=%async_computation.7 | async-start | bytes 1048576 | tf_op jit(solution)/shard_map/all_to_all | solution.py:220
Sparse Core Ops, SparseCore 0:
  38.9 46.1 all-reduce.6
  155.0 23.7 reduce-scatter.3
  210.1 14.2 reduce-scatter.5
  336.6 22.2 reduce-scatter.7
where the time goes:
time: 404 us; the launch traced here: 403 us
  waiting for transfers between devices  136 us (34%)
  blocking collectives  113 us (28%)
  starting transfers between devices  50.9 us (13%)
  local copies, waits for them, and re-layouts  43.6 us (11%)
  matrix products  30 us (7%)
  other arithmetic  14.6 us (4%)
  between operations  14.4 us (4%)
    all_to_all x1, blocking collectives, body(): lax.all_to_all(padded_rows[source_token].reshape(expert_count, capacity,...  70.5 us
    psum x1, waiting for transfers between devices, body(): lax.psum(jnp.dot(normed_part, w_latent, preferred_element_type=jnp.float3...  40.8 us
    reduce_scatter x1, waiting for transfers between devices, body(): lax.psum_scatter(jnp.dot(activity, expert_down[0], preferred_element_type...  21.5 us
    reduce_scatter x1, waiting for transfers between devices, body(): lax.psum_scatter(jnp.concatenate([numerator, denominator[:, :, None]], ax...  21 us
    all_to_all x1, waiting for transfers between devices, body(): got_packed = lax.all_to_all(packed[sent_row], 'tok', 0, 0, tiled=True)  15.7 us
    all_to_all x1, waiting for transfers between devices, body(): lax.all_to_all(expert_share.reshape(peer_count, capacity, quarter_width),...  15.5 us
    reduce_scatter x1, waiting for transfers between devices, body(): lax.psum_scatter(jnp.dot(head_out, w_out, preferred_element_type=jnp.floa...  14 us
    all_to_all x1, starting transfers between devices, body(): got_ints = lax.all_to_all(send_ints, 'tok', 0, 0, tiled=True)  13.1 us
  transfers between devices with their start and end apart: 8, of which 7 were waited for; matrix products, arithmetic and copies ran while one was open for 5% of the time, Pallas kernels for 0%

commit v1 on v0

--- a/solution.py
+++ b/solution.py
@@ -2,6 +2,7 @@
 import jax.numpy as jnp
 from jax import lax
 from jax.sharding import PartitionSpec as P
+from jax.lax import all_gather
 
 D = 2048
 NOPE = 128
@@ -81,8 +82,11 @@
     normed_part = lax.dynamic_slice_in_dim(
         normed_attn, head_index * quarter_width, quarter_width, 1
     )
-    compressed = lax.psum(
-        jnp.dot(normed_part, w_latent, preferred_element_type=jnp.float32), "head"
+    compressed = jnp.sum(
+        all_gather(
+            jnp.dot(normed_part, w_latent, preferred_element_type=jnp.float32), axis_name="head"
+        ),
+        axis=0,
     )
     latent_new = compressed[:, :LATENT]
     latent_new = latent_new * lax.rsqrt(

time: 404 us -> 378 us (0.936)
  waiting for transfers between devices: 136 us -> 93.7 us
  blocking collectives: 113 us -> 123 us
    psum x1 -> x0, waiting for transfers between devices: 40.8 us -> none  [body(): lax.psum(jnp.dot(normed_part, w_latent, preferred_element_type=jnp.float3...]
    all_gather x0 -> x1, blocking collectives: none -> 9.51 us  [body(): all_gather(jnp.dot(normed_part, w_latent, preferred_element_type=jnp.floa...]
  transfers between devices with their start and end apart: 8 -> 7, of which waited for: 7 -> 6; matrix products, arithmetic and copies ran while one was open for 5% -> 7% of each run, Pallas kernels for 0% -> 0%
where the time goes in v1:
time: 378 us; the launch traced here: 376 us
  blocking collectives  123 us (33%)
  waiting for transfers between devices  93.7 us (25%)
  starting transfers between devices  53.9 us (14%)
  local copies, waits for them, and re-layouts  46.8 us (12%)
  matrix products  29.4 us (8%)
  other arithmetic  15.4 us (4%)
  between operations  14.3 us (4%)
    all_to_all x1, blocking collectives, body(): lax.all_to_all(padded_rows[source_token].reshape(expert_count, capacity,...  70.5 us
    reduce_scatter x1, waiting for transfers between devices, body(): lax.psum_scatter(jnp.concatenate([numerator, denominator[:, :, None]], ax...  21.1 us
    reduce_scatter x1, waiting for transfers between devices, body(): lax.psum_scatter(jnp.dot(activity, expert_down[0], preferred_element_type...  20.8 us
    all_to_all x1, waiting for transfers between devices, body(): lax.all_to_all(expert_share.reshape(peer_count, capacity, quarter_width),...  16.2 us
    all_to_all x1, starting transfers between devices, body(): got_packed = lax.all_to_all(packed[sent_row], 'tok', 0, 0, tiled=True)  15.6 us
    reduce_scatter x1, waiting for transfers between devices, body(): lax.psum_scatter(jnp.dot(head_out, w_out, preferred_element_type=jnp.floa...  14 us
    all_to_all x1, waiting for transfers between devices, body(): got_packed = lax.all_to_all(packed[sent_row], 'tok', 0, 0, tiled=True)  13.9 us
    all_to_all x1, starting transfers between devices, body(): got_ints = lax.all_to_all(send_ints, 'tok', 0, 0, tiled=True)  13.3 us
  transfers between devices with their start and end apart: 7, of which 6 were waited for; matrix products, arithmetic and copies ran while one was open for 7% of the time, Pallas kernels for 0%

profile of v1, /device:TPU:1, one launch (start us, length us, event | category | flops | bytes accessed | tf_op | source)
XLA Modules:
  0.0 376.2 jit_solution(5864585484302895217)
XLA Ops:
  7.2 1.3 compare_select_fusion.3
  9.1 1.4 gather_fusion
  10.6 1.4 gather_fusion.1
  12.0 0.7 copy.107
  12.7 13.3 %all-to-all-start = ((s32[64,1,2]{2,1,0:T(1,128)}), s32[64,1,2]{2,1,0:T(1,128)}, u32[]{:S(2)}, u32[]{:S(2)}) async-start(s32[64,1,2]{2,1,0:T(1,128)} %copy.107), calls=%async_computation | async-start | bytes 65536 | tf_op jit(solution)/shard_map/all_to_all | solution.py:125
  26.1 1.2 convert_element_type.98
  27.8 10.5 %all_gather.15 = bf16[32,2048]{1,0:T(8,128)(2,1)S(1)} all-gather(bf16[32,512]{1,0:T(8,128)(2,1)} %param.16), channel_id=1, replica_groups=mesh['tok'=64,'head'=4] {'head'}, dimensions={1}, use_global_device_ids=true | all-gather | bytes 163840 | tf_op jit(solution)/shard_map/all_gather | solution.py:78
  38.5 0.8 fusion.28
  40.0 0.6 slice.82
  41.9 1.3 fusion.45
  43.2 9.5 %all-gather = f32[128,576]{1,0:T(8,128)S(1)} all-gather(f32[32,576]{1,0:T(8,128)S(1)} %fusion.45), channel_id=2, replica_groups=mesh['tok'=64,'head'=4] {'head'}, dimensions={0}, use_global_device_ids=true | all-gather | bytes 368640 | tf_op jit(solution)/shard_map/all_gather | solution.py:86
  53.0 1.3 fusion.16
  54.3 0.8 multiply_cosine_fusion
  55.1 1.0 subtract_convert_fusion
  56.8 0.8 copy.135
  57.6 1.0 concatenate.52.clone
  58.7 1.6 gather_fusion.3
  60.3 15.6 %all-to-all-start.1 = ((bf16[64,5,576]{2,1,0:T(8,128)(2,1)}), bf16[64,5,576]{2,1,0:T(8,128)(2,1)}, u32[]{:S(2)}, u32[]{:S(2)}) async-start(bf16[64,5,576]{2,1,0:T(8,128)(2,1)} %gather_fusion.3), calls=%async_computation.1 | async-start | bytes 1310720 | tf_op jit(solution)/shard_map/all_to_all | solution.py:124
  76.0 0.8 copy.108
  77.4 0.8 gather_fusion.2
  79.0 2.5 copy.117
  82.0 13.9 %all-to-all-done.1 = bf16[64,5,576]{2,1,0:T(8,128)(2,1)} async-done(((bf16[64,5,576]{2,1,0:T(8,128)(2,1)}), bf16[64,5,576]{2,1,0:T(8,128)(2,1)}, u32[]{:S(2)}, u32[]{:S(2)}) %all-to-all-start.1) | async-done | bytes 368672 | tf_op jit(solution)/shard_map/all_to_all | solution.py:124
  95.9 1.8 gather_fusion.4
  97.9 0.6 copy-done.6
  98.5 11.4 %all_gather.18 = bf16[32,16,576]{2,0,1:T(8,128)(2,1)S(1)} all-gather(bf16[32,4,576]{2,0,1:T(8,128)(2,1)S(1)} %copy.113), channel_id=1, replica_groups=mesh['tok'=64,'head'=4] {'head'}, dimensions={1}, use_global_device_ids=true | all-gather | bytes 737280 | tf_op jit(solution)/shard_map/all_gather | solution.py:134
  110.2 6.9 %convert_reduce_fusion = (f32[512]{0:T(512)}, bf16[512,2496]{0,1:T(8,128)(2,1)}) fusion(pred[512,2496]{0,1:T(32,128)(4,1)S(1)} %copy-done.1, bf16[512,576]{1,0:T(8,128)(2,1)S(1)} %bitcast.108, bf16[2496,576]{0,1:T(8,128)(2,1)} %param.23), kind=kOutput, calls=%fused_computation.11 | convolution fusion | flops 1478589952 | bytes 7301120 | tf_op jit(solution)/shard_map/qc,pc->qp/dot_general | solution.py:38
  117.1 0.9 broadcast_in_dim.142
  118.0 4.4 %copy.115 = bf16[512,2496]{1,0:T(8,128)(2,1)} copy(bf16[512,2496]{0,1:T(8,128)(2,1)} %get-tuple-element.32) | data formatting | bytes 5111808 | tf_op jit(solution)/shard_map/exp | solution.py:45
  122.4 4.1 %fusion = f32[32,16,512]{2,1,0:T(8,128)S(1)} fusion(bf16[32,16,2496]{2,1,0:T(8,128)(2,1)} %bitcast.105, bf16[2496,576]{0,1:T(8,128)(2,1)} %param.23, pred[32,2496]{1,0:T(8,128)(4,1)S(1)} %compare_and_fusion), kind=kOutput, calls=%fused_computation.15 | convolution fusion | flops 1309900800 | bytes 6371328 | tf_op jit(solution)/shard_map/khp,pl->khl/dot_general | solution.py:46
  126.6 1.5 copy.119
  128.4 1.8 fusion.35
  130.2 0.8 copy.129
  131.0 21.1 %reduce-scatter.4.cloned.1.call-done = f32[32,4,513]{2,0,1:T(8,128)} async-done(((f32[32,16,513]{2,0,1:T(8,128)}), f32[32,4,513]{2,0,1:T(8,128)}) %reduce-scatter.4.cloned.1.call-update) | async-done | bytes 262672 | tf_op jit(solution)/shard_map/reduce_scatter | solution.py:138
  152.1 0.9 slice_reduce_fusion
  153.0 1.4 fusion.17
  154.5 0.7 gather_fusion.5
  155.7 0.7 reduce.6
  156.4 0.7 reshape.502
  157.0 13.1 %all-to-all-start.2 = ((bf16[64,2,256]{2,1,0:T(2,128)(2,1)}), bf16[64,2,256]{2,1,0:T(2,128)(2,1)S(1)}, u32[]{:S(2)}, u32[]{:S(2)}) async-start(bf16[64,2,256]{2,1,0:T(2,128)(2,1)} %reshape.502), calls=%async_computation.3 | async-start | bytes 131072 | tf_op jit(solution)/shard_map/all_to_all | solution.py:164
  170.4 1.6 gather_fusion.9
  172.1 7.7 %all-to-all-done.2 = bf16[64,2,256]{2,1,0:T(2,128)(2,1)S(1)} async-done(((bf16[64,2,256]{2,1,0:T(2,128)(2,1)}), bf16[64,2,256]{2,1,0:T(2,128)(2,1)S(1)}, u32[]{:S(2)}, u32[]{:S(2)}) %all-to-all-start.2) | async-done | bytes 65568 | tf_op jit(solution)/shard_map/all_to_all | solution.py:164
  180.0 0.6 gather_fusion.6
  180.6 2.8 fusion.62
  183.7 14.0 %reduce-scatter.6.cloned.1.call-done = f32[32,512]{1,0:T(8,128)} async-done(((f32[32,2048]{1,0:T(8,128)}), f32[32,512]{1,0:T(8,128)}) %reduce-scatter.6.cloned.1.call-update) | async-done | bytes 65552 | tf_op jit(solution)/shard_map/reduce_scatter | solution.py:167
  197.7 1.0 fusion.40
  198.9 11.8 %all-reduce.4 = (f32[32]{0:T(128)S(1)}, f32[32,64]{1,0:T(8,128)S(1)}) all-reduce(f32[32]{0:T(128)S(1)} %get-tuple-element.11, f32[32,64]{1,0:T(8,128)S(1)} %fusion.41), channel_id=1, replica_groups=mesh['tok'=64,'head'=4] {'head'}, use_global_device_ids=true, to_apply=%region_12.13 | all-reduce | flops 2080 | bytes 16640 | tf_op jit(solution)/shard_map/psum | solution.py:176
  210.7 9.1 %all_gather.19 = bf16[32,2048]{1,0:T(8,128)(2,1)S(1)} all-gather(bf16[32,512]{1,0:T(8,128)(2,1)S(1)} %fusion.39), channel_id=1, replica_groups=mesh['tok'=64,'head'=4] {'head'}, dimensions={1}, use_global_device_ids=true | all-gather | bytes 163840 | tf_op jit(solution)/shard_map/all_gather | solution.py:203
  219.9 3.1 gather_fusion.7
  223.0 3.7 reshape.405
  226.6 70.5 %all_to_all.39 = bf16[64,6,2048]{2,1,0:T(8,128)(2,1)} all-to-all(bf16[64,6,2048]{2,1,0:T(8,128)(2,1)} %reshape.405), channel_id=1, replica_groups=mesh['tok'=64,'head'=4] {'tok'}, dimensions={0} | all-to-all | bytes 3145728 | tf_op jit(solution)/shard_map/all_to_all | solution.py:207
  297.1 3.7 reshape.406
  300.8 3.6 fusion.8
  304.4 5.5 %convolution_convert_fusion = bf16[384,2048]{1,0:T(8,128)(2,1)} fusion(bf16[1,352,2048]{2,1,0:T(8,128)(2,1)} %param.31, bf16[384,2048]{1,0:T(8,128)(2,1)} %reshape.406, bf16[1,2048,352]{1,2,0:T(8,128)(2,1)} %param.30, f32[384,352]{0,1:T(8,128)} %fusion.8), kind=kOutput, calls=%fused_computation.14 | convolution fusion | flops 1108893696 | bytes 6569984 | tf_op jit(solution)/shard_map/dot_general | solution.py:219
  310.0 0.7 copy-done.3
  310.9 0.7 pad_maximum_fusion.1
  311.6 20.8 %reduce-scatter.8.cloned.1.call-done = bf16[384,512]{1,0:T(8,128)(2,1)} async-done(((bf16[384,2048]{1,0:T(8,128)(2,1)}), bf16[384,512]{1,0:T(8,128)(2,1)}) %reduce-scatter.8.cloned.1.call-update) | async-done | bytes 393232 | tf_op jit(solution)/shard_map/reduce_scatter | solution.py:218
  332.3 1.9 reshape.407
  334.2 11.7 %all-to-all-start.4 = ((bf16[64,6,512]{2,1,0:T(8,128)(2,1)}), bf16[64,6,512]{2,1,0:T(8,128)(2,1)}, u32[]{:S(2)}, u32[]{:S(2)}) async-start(bf16[64,6,512]{2,1,0:T(8,128)(2,1)} %reshape.407), calls=%async_computation.7 | async-start | bytes 1048576 | tf_op jit(solution)/shard_map/all_to_all | solution.py:224
  346.3 0.7 copy.122
  347.0 16.2 %all-to-all-done.4 = bf16[64,6,512]{2,1,0:T(8,128)(2,1)} async-done(((bf16[64,6,512]{2,1,0:T(8,128)(2,1)}), bf16[64,6,512]{2,1,0:T(8,128)(2,1)}, u32[]{:S(2)}, u32[]{:S(2)}) %all-to-all-start.4) | async-done | bytes 393248 | tf_op jit(solution)/shard_map/all_to_all | solution.py:224
  363.2 1.2 reshape.408
  364.4 1.7 gather_fusion.8
  366.0 1.8 reshape.489
  367.8 1.9 multiply_reduce_fusion
  (117 shorter events, 9.0 us)
Async XLA Ops:
  7.2 32.1 %copy-start = (bf16[2048,768]{1,0:T(8,128)(2,1)S(1)}, bf16[2048,768]{1,0:T(8,128)(2,1)}, u32[]{:S(2)}) copy-start(bf16[2048,768]{1,0:T(8,128)(2,1)} %param.18) | copy-start | bytes 9437188
  12.7 47.6 %all-to-all-start = ((s32[64,1,2]{2,1,0:T(1,128)}), s32[64,1,2]{2,1,0:T(1,128)}, u32[]{:S(2)}, u32[]{:S(2)}) async-start(s32[64,1,2]{2,1,0:T(1,128)} %copy.107), calls=%async_computation | async-start | bytes 65536 | tf_op jit(solution)/shard_map/all_to_all | solution.py:125
  52.8 4.9 %copy-start.2 = (f32[32,576]{1,0:T(8,128)}, f32[32,576]{1,0:T(8,128)S(1)}, u32[]{:S(2)}) copy-start(f32[32,576]{1,0:T(8,128)S(1)} %reduce_sum.102) | copy-start | bytes 221188
  52.8 3.4 copy-start.19
  52.9 2.2 copy-start.17
  55.1 2.6 copy-start.9
  55.1 2.5 copy-start.11
  60.3 18.2 %copy-start.14 = (s32[2496]{0:T(1024)S(1)}, s32[2496]{0:T(1024)}, u32[]{:S(2)}) copy-start(s32[2496]{0:T(1024)} %iota_add_fusion) | copy-start | bytes 29956
  60.3 35.6 %all-to-all-start.1 = ((bf16[64,5,576]{2,1,0:T(8,128)(2,1)}), bf16[64,5,576]{2,1,0:T(8,128)(2,1)}, u32[]{:S(2)}, u32[]{:S(2)}) async-start(bf16[64,5,576]{2,1,0:T(8,128)(2,1)} %gather_fusion.3), calls=%async_computation.1 | async-start | bytes 1310720 | tf_op jit(solution)/shard_map/all_to_all | solution.py:124
  75.9 76.2 %reduce-scatter.4.cloned.1.call-start = ((), (), s32[]{:S(2)}) async-start(), calls=%async_computation.8 | async-start | bytes 1638400 | tf_op jit(solution)/shard_map/reduce_scatter | solution.py:138
  97.8 19.3 %copy-start.4 = (bf16[32,5,576]{2,1,0:T(8,128)(2,1)}, bf16[32,5,576]{2,1,0:T(8,128)(2,1)S(1)}, u32[]{:S(2)}) copy-start(bf16[32,5,576]{2,1,0:T(8,128)(2,1)S(1)} %gather_fusion.4) | copy-start | bytes 552964
  97.8 12.4 %copy-start.1 = (pred[512,2496]{0,1:T(32,128)(4,1)S(1)}, pred[512,2496]{0,1:T(32,128)(4,1)}, u32[]{:S(2)}) copy-start(pred[512,2496]{0,1:T(32,128)(4,1)} %copy.117) | copy-start | bytes 3833860
  97.9 0.7 copy-start.6
  126.6 1.5 copy-start.15
  126.6 1.6 copy-start.20
  126.6 1.6 copy-start.5
  157.0 22.8 %all-to-all-start.2 = ((bf16[64,2,256]{2,1,0:T(2,128)(2,1)}), bf16[64,2,256]{2,1,0:T(2,128)(2,1)S(1)}, u32[]{:S(2)}, u32[]{:S(2)}) async-start(bf16[64,2,256]{2,1,0:T(2,128)(2,1)} %reshape.502), calls=%async_computation.3 | async-start | bytes 131072 | tf_op jit(solution)/shard_map/all_to_all | solution.py:164
  170.1 27.7 %reduce-scatter.6.cloned.1.call-start = ((), (), s32[]{:S(2)}) async-start(), calls=%async_computation.9 | async-start | bytes 327680 | tf_op jit(solution)/shard_map/reduce_scatter | solution.py:167
  170.4 1.7 copy-start.21
  179.9 17.8 %copy-start.8 = (bf16[32,512]{1,0:T(8,128)(2,1)S(1)}, bf16[32,512]{1,0:T(8,128)(2,1)}, u32[]{:S(2)}) copy-start(bf16[32,512]{1,0:T(8,128)(2,1)} %param.16) | copy-start | bytes 98308
  179.9 18.8 %copy-start.13 = (bf16[512,64]{0,1:T(8,128)(2,1)S(1)}, bf16[512,64]{0,1:T(8,128)(2,1)}, u32[]{:S(2)}) copy-start(bf16[512,64]{0,1:T(8,128)(2,1)} %param.27) | copy-start | bytes 196612
  179.9 18.8 %copy-start.16 = (f32[512]{0:T(512)S(1)}, f32[512]{0:T(512)}, u32[]{:S(2)}) copy-start(f32[512]{0:T(512)} %param.26) | copy-start | bytes 6148
  183.4 149.0 %reduce-scatter.8.cloned.1.call-start = ((), (), s32[]{:S(2)}) async-start(), calls=%async_computation.10 | async-start | bytes 1966080 | tf_op jit(solution)/shard_map/reduce_scatter | solution.py:218
  198.7 12.0 %copy-start.7 = (bf16[32,512]{1,0:T(8,128)(2,1)}, bf16[32,512]{1,0:T(8,128)(2,1)S(1)}, u32[]{:S(2)}) copy-start(bf16[32,512]{1,0:T(8,128)(2,1)S(1)} %get-tuple-element.12) | copy-start | bytes 98308
  309.9 0.9 copy-start.3
  309.9 0.9 copy-start.18
  309.9 1.0 copy-start.10
  309.9 1.0 copy-start.12
  334.2 28.9 %all-to-all-start.4 = ((bf16[64,6,512]{2,1,0:T(8,128)(2,1)}), bf16[64,6,512]{2,1,0:T(8,128)(2,1)}, u32[]{:S(2)}, u32[]{:S(2)}) async-start(bf16[64,6,512]{2,1,0:T(8,128)(2,1)} %reshape.407), calls=%async_computation.7 | async-start | bytes 1048576 | tf_op jit(solution)/shard_map/all_to_all | solution.py:224
Sparse Core Ops, SparseCore 0:
  128.3 23.7 reduce-scatter.3
  183.5 14.2 reduce-scatter.5
  310.1 22.2 reduce-scatter.7
